TPU v7x, 256 devices: a whole 4x4x8 slice. The times are simulated.
256 devices in a mesh: gz: 32 (over z, y_hi, core), ch: 8 (over y_lo, x).
Axes of the slice: x: 4, y: 4 (y_hi: 2, y_lo: 2; y = y_hi * 2 + y_lo), z: 8, core: 2. Of those that a mesh axis runs over, the one named last changes fastest.
Arguments:
- volume: bfloat16 [64, 1024, 512], P('ch', 'gz'), may hold values from -6 to 6
- plane_a: bfloat16 [2, 64, 64, 3, 3], P(None, 'ch'), may hold values from -0.375 to 0.375
- plane_b: bfloat16 [2, 64, 64, 3, 3], P(None, 'ch'), may hold values from -0.375 to 0.375
- depth: bfloat16 [2, 64, 64, 3], P(None, 'ch'), may hold values from -0.625 to 0.625
Outputs:
- features: bfloat16 [64, 1024, 512], P('ch', 'gz')
All inputs are finite; a program needn't handle non-finite values.
Results may differ from a plain program's by a relative error of at most 0.015.
Values may be sent and summed in bfloat16 or wider, within the bound.
No kernel may reach another device: no remote copies, remote signals or barrier semaphores. Data moves between devices by JAX's collectives and lax.ppermute only.
A program may use at most 64 MiB of HBM per device.

v0:
```python
import jax
import jax.numpy as jnp
from jax import lax
from jax.sharding import PartitionSpec as P

X = 64
Y = 8


def from_behind(block, axis, distance):
    devices = range(lax.axis_size(axis))
    route = [(i - distance, i) for i in devices if i - distance in devices]
    return lax.ppermute(block, axis, route)


def gather_weights(plane_a, plane_b, depth):
    return (
        lax.all_gather(plane_a, "ch", axis=1, tiled=True),
        lax.all_gather(plane_b, "ch", axis=1, tiled=True),
        lax.all_gather(depth, "ch", axis=1, tiled=True),
    )


def plane_conv(h, weight):
    out = lax.conv_general_dilated(
        h,
        weight,
        (1, 1),
        ((1, 1), (1, 1)),
        dimension_numbers=("CNHW", "OIHW", "CNHW"),
        preferred_element_type=jnp.float32,
    )
    return jnp.maximum(out, 0.0).astype(jnp.bfloat16)


def depth_conv(second, weight):
    lower = from_behind(second, "gz", 2)
    upper = from_behind(second, "gz", -2)
    total = jnp.einsum("oi,isxy->osxy", weight[:, :, 1], second, preferred_element_type=jnp.float32)
    total = total + jnp.einsum(
        "oi,isxy->osxy", weight[:, :, 0], lower, preferred_element_type=jnp.float32
    )
    total = total + jnp.einsum(
        "oi,isxy->osxy", weight[:, :, 2], upper, preferred_element_type=jnp.float32
    )
    return jnp.maximum(total, 0.0).astype(jnp.bfloat16)


def local(volume, plane_a, plane_b, depth):
    full_a, full_b, full_d = gather_weights(plane_a, plane_b, depth)
    part, slab, flat = volume.shape
    h = lax.all_to_all(volume, "ch", split_axis=1, concat_axis=0, tiled=True)
    chans, slices = h.shape[:2]
    h = h.reshape(chans, slices, X, Y)
    for layer_index in range(plane_a.shape[0]):
        first = plane_conv(h, full_a[layer_index])
        second = plane_conv(first, full_b[layer_index])
        h = depth_conv(second, full_d[layer_index])
    h = h.reshape(chans, slices, flat)
    return lax.all_to_all(h, "ch", split_axis=0, concat_axis=1, tiled=True)


def solution(mesh):
    return jax.shard_map(
        local,
        mesh=mesh,
        in_specs=(
            P("ch", "gz", None),
            P(None, "ch", None, None, None),
            P(None, "ch", None, None, None),
            P(None, "ch", None, None),
        ),
        out_specs=P("ch", "gz", None),
        check_vma=False,
    )
```

profile of v0, /device:TPU:96, one launch (start us, length us, event | category | flops | bytes accessed | tf_op | source)
XLA Modules:
  0.0 164.3 jit_solution(17486440112829499366)
XLA Ops:
  0.0 1.8 %copy.37 = bf16[8,32,512]{2,0,1:T(8,128)(2,1)} copy(bf16[8,32,512]{2,1,0:T(8,128)(2,1)} %param.4) | data formatting | bytes 524288 | tf_op args[0]
  1.8 5.3 %all-to-all-start = ((bf16[8,32,512]{2,0,1:T(8,128)(2,1)}), bf16[8,32,512]{2,0,1:T(8,128)(2,1)S(1)}, u32[]{:S(2)}, u32[]{:S(2)}) async-start(bf16[8,32,512]{2,0,1:T(8,128)(2,1)} %copy.37), calls=%async_computation | async-start | bytes 524288 | tf_op jit(solution)/shard_map/all_to_all | solution.py:52
  7.1 25.9 %all_gather.10 = bf16[2,64,64,3,3]{2,1,4,3,0:T(8,128)(2,1)S(1)} all-gather(bf16[2,8,64,3,3]{2,1,4,3,0:T(8,128)(2,1)} %param.6), channel_id=1, replica_groups=mesh['gz'=32,'ch'=8] {'ch'}, dimensions={1}, use_global_device_ids=true | all-gather | bytes 165888 | tf_op jit(solution)/shard_map/all_gather | solution.py:19
  33.0 24.8 %all_gather.9 = bf16[2,64,64,3,3]{2,1,4,3,0:T(8,128)(2,1)S(1)} all-gather(bf16[2,8,64,3,3]{2,1,4,3,0:T(8,128)(2,1)} %param.5), channel_id=1, replica_groups=mesh['gz'=32,'ch'=8] {'ch'}, dimensions={1}, use_global_device_ids=true | all-gather | bytes 165888 | tf_op jit(solution)/shard_map/all_gather | solution.py:18
  57.9 23.9 %all_gather.11 = bf16[2,64,64,3]{2,1,3,0:T(8,128)(2,1)S(1)} all-gather(bf16[2,8,64,3]{2,1,3,0:T(8,128)(2,1)} %param.7), channel_id=1, replica_groups=mesh['gz'=32,'ch'=8] {'ch'}, dimensions={1}, use_global_device_ids=true | all-gather | bytes 55296 | tf_op jit(solution)/shard_map/all_gather | solution.py:20
  81.8 0.0 all-to-all-done
  81.8 5.9 %reshape.7 = bf16[64,4,64,8]{3,2,0,1:T(8,128)(2,1)} reshape(bf16[8,8,4,512]{3,1,0,2:T(8,128)(2,1)S(1)} %bitcast.81) | data formatting | bytes 524288 | tf_op jit(solution)/shard_map/reshape | solution.py:54
  87.7 5.7 %copy.39 = bf16[64,4,64,8]{0,1,3,2:T(4,128)(2,1)S(1)} copy(bf16[64,4,64,8]{3,2,0,1:T(8,128)(2,1)} %reshape.7) | data formatting | bytes 524288 | tf_op jit(solution)/shard_map/reshape | solution.py:54
  93.4 5.5 %fusion.5 = bf16[64,4,64,8]{0,1,3,2:T(4,128)(2,1)S(1)} fusion(bf16[64,4,64,8]{0,1,3,2:T(4,128)(2,1)S(1)} %copy.39, bf16[2,64,64,3,3]{2,1,4,3,0:T(8,128)(2,1)S(1)} %all_gather.10, bf16[2,64,64,3,3]{2,1,4,3,0:T(8,128)(2,1)S(1)} %all_gather.9), kind=kOutput, calls=%fused_computation.13 | convolution fusion | flops 274464768 | bytes 1081344 | tf_op jit(solution)/shard_map/conv_general_dilated | solution.py:25
  98.8 4.8 %collective-permute-start = (bf16[64,4,64,8]{0,1,3,2:T(4,128)(2,1)S(1)}, bf16[64,4,64,8]{0,1,3,2:T(4,128)(2,1)S(1)}, u32[]{:S(2)}, u32[]{:S(2)}) collective-permute-start(bf16[64,4,64,8]{0,1,3,2:T(4,128)(2,1)S(1)} %fusion.5), channel_id=1, source_target_pairs={{0,16},{8,24},{16,32},{24,40},{32,48},{40,56},{48,64},{56,72},{64,... | collective-permute-start | bytes 786440 | tf_op jit(solution)/shard_map/ppermute | solution.py:13
  103.7 3.6 %collective-permute-start.1 = (bf16[64,4,64,8]{0,1,3,2:T(4,128)(2,1)S(1)}, bf16[64,4,64,8]{0,1,3,2:T(4,128)(2,1)S(1)}, u32[]{:S(2)}, u32[]{:S(2)}) collective-permute-start(bf16[64,4,64,8]{0,1,3,2:T(4,128)(2,1)S(1)} %fusion.5), channel_id=1, source_target_pairs={{16,0},{24,8},{32,16},{40,24},{48,32},{56,40},{64,48},{72,56},{80,... | collective-permute-start | bytes 786440 | tf_op jit(solution)/shard_map/ppermute | solution.py:13
  107.3 0.4 fusion.16
  107.7 4.7 %collective-permute-done = bf16[64,4,64,8]{0,1,3,2:T(4,128)(2,1)S(1)} collective-permute-done((bf16[64,4,64,8]{0,1,3,2:T(4,128)(2,1)S(1)}, bf16[64,4,64,8]{0,1,3,2:T(4,128)(2,1)S(1)}, u32[]{:S(2)}, u32[]{:S(2)}) %collective-permute-start) | collective-permute-done | bytes 262176 | tf_op jit(solution)/shard_map/ppermute | solution.py:13
  112.4 0.4 convolution_add_fusion.3
  112.8 12.6 %collective-permute-done.1 = bf16[64,4,64,8]{0,1,3,2:T(4,128)(2,1)S(1)} collective-permute-done((bf16[64,4,64,8]{0,1,3,2:T(4,128)(2,1)S(1)}, bf16[64,4,64,8]{0,1,3,2:T(4,128)(2,1)S(1)}, u32[]{:S(2)}, u32[]{:S(2)}) %collective-permute-start.1) | collective-permute-done | bytes 262176 | tf_op jit(solution)/shard_map/ppermute | solution.py:13
  125.5 0.4 fusion.2
  125.9 5.5 %fusion.7 = bf16[64,4,64,8]{0,1,3,2:T(4,128)(2,1)S(1)} fusion(bf16[4,64,8,64]{3,1,2,0:T(8,128)(2,1)S(1)} %fusion.2, bf16[2,64,64,3,3]{2,1,4,3,0:T(8,128)(2,1)S(1)} %all_gather.10, bf16[2,64,64,3,3]{2,1,4,3,0:T(8,128)(2,1)S(1)} %all_gather.9), kind=kOutput, calls=%fused_computation.15 | convolution fusion | flops 274464768 | bytes 1081344 | tf_op jit(solution)/shard_map/conv_general_dilated | solution.py:25
  131.4 1.9 %collective-permute-start.2 = (bf16[64,4,64,8]{0,1,3,2:T(4,128)(2,1)S(1)}, bf16[64,4,64,8]{0,1,3,2:T(4,128)(2,1)S(1)}, u32[]{:S(2)}, u32[]{:S(2)}) collective-permute-start(bf16[64,4,64,8]{0,1,3,2:T(4,128)(2,1)S(1)} %fusion.7), channel_id=1, source_target_pairs={{0,16},{8,24},{16,32},{24,40},{32,48},{40,56},{48,64},{56,72},{64,... | collective-permute-start | bytes 786440 | tf_op jit(solution)/shard_map/ppermute | solution.py:13
  133.4 6.3 %collective-permute-start.3 = (bf16[64,4,64,8]{0,1,3,2:T(4,128)(2,1)S(1)}, bf16[64,4,64,8]{0,1,3,2:T(4,128)(2,1)S(1)}, u32[]{:S(2)}, u32[]{:S(2)}) collective-permute-start(bf16[64,4,64,8]{0,1,3,2:T(4,128)(2,1)S(1)} %fusion.7), channel_id=1, source_target_pairs={{16,0},{24,8},{32,16},{40,24},{48,32},{56,40},{64,48},{72,56},{80,... | collective-permute-start | bytes 786440 | tf_op jit(solution)/shard_map/ppermute | solution.py:13
  139.7 0.4 fusion.11
  140.1 6.0 %collective-permute-done.2 = bf16[64,4,64,8]{0,1,3,2:T(4,128)(2,1)S(1)} collective-permute-done((bf16[64,4,64,8]{0,1,3,2:T(4,128)(2,1)S(1)}, bf16[64,4,64,8]{0,1,3,2:T(4,128)(2,1)S(1)}, u32[]{:S(2)}, u32[]{:S(2)}) %collective-permute-start.2) | collective-permute-done | bytes 262176 | tf_op jit(solution)/shard_map/ppermute | solution.py:13
  146.1 0.4 convolution_add_fusion.1
  146.5 5.1 %collective-permute-done.3 = bf16[64,4,64,8]{0,1,3,2:T(4,128)(2,1)S(1)} collective-permute-done((bf16[64,4,64,8]{0,1,3,2:T(4,128)(2,1)S(1)}, bf16[64,4,64,8]{0,1,3,2:T(4,128)(2,1)S(1)}, u32[]{:S(2)}, u32[]{:S(2)}) %collective-permute-start.3) | collective-permute-done | bytes 262176 | tf_op jit(solution)/shard_map/ppermute | solution.py:13
  151.6 0.4 fusion.8
  152.0 0.3 copy.77
  152.4 0.3 copy.48
  152.6 10.8 %all_to_all.33 = bf16[64,4,512]{2,1,0:T(4,128)(2,1)S(1)} all-to-all(bf16[64,4,512]{2,1,0:T(4,128)(2,1)S(1)} %copy.48), channel_id=1, replica_groups=mesh['gz'=32,'ch'=8] {'ch'}, dimensions={0} | all-to-all | bytes 524288 | tf_op jit(solution)/shard_map/all_to_all | solution.py:60
  163.5 0.8 copy.51
  (4 shorter events, 0.1 us)
Async XLA Ops:
  1.8 80.0 %all-to-all-start = ((bf16[8,32,512]{2,0,1:T(8,128)(2,1)}), bf16[8,32,512]{2,0,1:T(8,128)(2,1)S(1)}, u32[]{:S(2)}, u32[]{:S(2)}) async-start(bf16[8,32,512]{2,0,1:T(8,128)(2,1)} %copy.37), calls=%async_computation | async-start | bytes 524288 | tf_op jit(solution)/shard_map/all_to_all | solution.py:52
  98.8 13.6 %collective-permute-start = (bf16[64,4,64,8]{0,1,3,2:T(4,128)(2,1)S(1)}, bf16[64,4,64,8]{0,1,3,2:T(4,128)(2,1)S(1)}, u32[]{:S(2)}, u32[]{:S(2)}) collective-permute-start(bf16[64,4,64,8]{0,1,3,2:T(4,128)(2,1)S(1)} %fusion.5), channel_id=1, source_target_pairs={{0,16},{8,24},{16,32},{24,40},{32,48},{40,56},{48,64},{56,72},{64,... | collective-permute-start | bytes 786440 | tf_op jit(solution)/shard_map/ppermute | solution.py:13
  103.7 21.8 %collective-permute-start.1 = (bf16[64,4,64,8]{0,1,3,2:T(4,128)(2,1)S(1)}, bf16[64,4,64,8]{0,1,3,2:T(4,128)(2,1)S(1)}, u32[]{:S(2)}, u32[]{:S(2)}) collective-permute-start(bf16[64,4,64,8]{0,1,3,2:T(4,128)(2,1)S(1)} %fusion.5), channel_id=1, source_target_pairs={{16,0},{24,8},{32,16},{40,24},{48,32},{56,40},{64,48},{72,56},{80,... | collective-permute-start | bytes 786440 | tf_op jit(solution)/shard_map/ppermute | solution.py:13
  131.4 14.6 %collective-permute-start.2 = (bf16[64,4,64,8]{0,1,3,2:T(4,128)(2,1)S(1)}, bf16[64,4,64,8]{0,1,3,2:T(4,128)(2,1)S(1)}, u32[]{:S(2)}, u32[]{:S(2)}) collective-permute-start(bf16[64,4,64,8]{0,1,3,2:T(4,128)(2,1)S(1)} %fusion.7), channel_id=1, source_target_pairs={{0,16},{8,24},{16,32},{24,40},{32,48},{40,56},{48,64},{56,72},{64,... | collective-permute-start | bytes 786440 | tf_op jit(solution)/shard_map/ppermute | solution.py:13
  133.4 18.2 %collective-permute-start.3 = (bf16[64,4,64,8]{0,1,3,2:T(4,128)(2,1)S(1)}, bf16[64,4,64,8]{0,1,3,2:T(4,128)(2,1)S(1)}, u32[]{:S(2)}, u32[]{:S(2)}) collective-permute-start(bf16[64,4,64,8]{0,1,3,2:T(4,128)(2,1)S(1)} %fusion.7), channel_id=1, source_target_pairs={{16,0},{24,8},{32,16},{40,24},{48,32},{56,40},{64,48},{72,56},{80,... | collective-permute-start | bytes 786440 | tf_op jit(solution)/shard_map/ppermute | solution.py:13
where the time goes:
time: 165 us; the launch traced here: 164 us
  blocking collectives  85.4 us (52%)
  waiting for transfers between devices  28.4 us (17%)
  starting transfers between devices  22 us (13%)
  local copies, waits for them, and re-layouts  14.9 us (9%)
  matrix products  13.4 us (8%)
    ppermute x4, waiting for transfers between devices, from_behind(): return lax.ppermute(block, axis, route)  28.4 us
    all_gather x1, blocking collectives, gather_weights(): lax.all_gather(plane_b, 'ch', axis=1, tiled=True)  25.9 us
    all_gather x1, blocking collectives, gather_weights(): lax.all_gather(plane_a, 'ch', axis=1, tiled=True)  24.8 us
    all_gather x1, blocking collectives, gather_weights(): lax.all_gather(depth, 'ch', axis=1, tiled=True)  23.9 us
    ppermute x4, starting transfers between devices, from_behind(): return lax.ppermute(block, axis, route)  16.7 us
    reshape x2, local copies, waits for them, and re-layouts, local(): h = h.reshape(chans, slices, X, Y)  11.6 us
    conv_general_dilated x2, matrix products, plane_conv(): lax.conv_general_dilated(h, weight, (1, 1), ((1, 1), (1, 1)), dimension_n...  11 us
    all_to_all x1, blocking collectives, local(): return lax.all_to_all(h, 'ch', split_axis=0, concat_axis=1, tiled=True)  10.8 us
  transfers between devices with their start and end apart: 5, of which 4 were waited for; matrix products, arithmetic and copies ran while one was open for 1% of the time, Pallas kernels for 0%

commit v1 on v0

--- a/solution.py
+++ b/solution.py
@@ -1,3 +1,4 @@
+import functools
 import jax
 import jax.numpy as jnp
 from jax import lax
@@ -5,6 +6,15 @@
 
 X = 64
 Y = 8
+
+
+def _serve_rows(field_in, row_axis):
+    then = jnp.stack(lax.axis_size(row_axis) * [field_in])
+    vec_out = lax.all_to_all(then, row_axis, 0, 0)
+    return jnp.concatenate(vec_out, 1)
+
+
+read_words = functools.partial(_serve_rows, row_axis="ch")
 
 
 def from_behind(block, axis, distance):
@@ -15,7 +25,7 @@
 
 def gather_weights(plane_a, plane_b, depth):
     return (
-        lax.all_gather(plane_a, "ch", axis=1, tiled=True),
+        read_words(plane_a),
         lax.all_gather(plane_b, "ch", axis=1, tiled=True),
         lax.all_gather(depth, "ch", axis=1, tiled=True),
     )

time: 165 us -> 147 us (0.89)
  the two profiles are of different devices: /device:TPU:96 before, /device:TPU:128 now
where the time goes in v1:
time: 147 us
  blocking collectives  59.9 us (41%)
  waiting for transfers between devices  28.2 us (19%)
  starting transfers between devices  27.8 us (19%)
  local copies, waits for them, and re-layouts  17 us (12%)
  matrix products  13.6 us (9%)
    all_gather x1, blocking collectives, gather_weights(): lax.all_gather(plane_b, 'ch', axis=1, tiled=True)  25.2 us
    all_gather x1, blocking collectives, gather_weights(): lax.all_gather(depth, 'ch', axis=1, tiled=True)  24.9 us
    ppermute x4, waiting for transfers between devices, from_behind(): return lax.ppermute(block, axis, route)  21.3 us
    ppermute x4, starting transfers between devices, from_behind(): return lax.ppermute(block, axis, route)  19.1 us
    reshape x2, local copies, waits for them, and re-layouts, local(): h = h.reshape(chans, slices, X, Y)  11.7 us
    conv_general_dilated x2, matrix products, plane_conv(): lax.conv_general_dilated(h, weight, (1, 1), ((1, 1), (1, 1)), dimension_n...  11.1 us
    all_to_all x1, blocking collectives, local(): return lax.all_to_all(h, 'ch', split_axis=0, concat_axis=1, tiled=True)  9.81 us
    all_to_all x1, waiting for transfers between devices, local(): h = lax.all_to_all(volume, 'ch', split_axis=1, concat_axis=0, tiled=True)  6.91 us
  transfers between devices with their start and end apart: 6, of which 5 were waited for; matrix products, arithmetic and copies ran while one was open for 3% of the time, Pallas kernels for 0%

profile of v1, /device:TPU:128, one launch (start us, length us, event | category | flops | bytes accessed | tf_op | source)
XLA Modules:
  0.0 146.6 jit_solution(15589182646225962946)
XLA Ops:
  0.0 0.8 copy-done
  0.8 0.9 reshape.26
  1.7 5.3 %all-to-all-start.1 = ((bf16[8,2,4608]{2,1,0:T(2,128)(2,1)}), bf16[8,2,4608]{2,1,0:T(2,128)(2,1)S(1)}, u32[]{:S(2)}, u32[]{:S(2)}) async-start(bf16[8,2,4608]{2,1,0:T(2,128)(2,1)} %reshape.26), calls=%async_computation.1 | async-start | bytes 294912 | tf_op jit(solution)/shard_map/all_to_all | solution.py:13
  7.0 24.9 %all_gather.7 = bf16[2,64,64,3]{2,1,3,0:T(8,128)(2,1)S(1)} all-gather(bf16[2,8,64,3]{2,1,3,0:T(8,128)(2,1)} %param.7), channel_id=1, replica_groups=mesh['gz'=32,'ch'=8] {'ch'}, dimensions={1}, use_global_device_ids=true | all-gather | bytes 55296 | tf_op jit(solution)/shard_map/all_gather | solution.py:30
  31.9 1.8 %copy.37 = bf16[8,32,512]{2,0,1:T(8,128)(2,1)} copy(bf16[8,32,512]{2,1,0:T(8,128)(2,1)} %param.4) | data formatting | bytes 524288 | tf_op args[0]
  33.7 25.2 %all_gather.6 = bf16[2,64,64,3,3]{2,1,4,3,0:T(8,128)(2,1)S(1)} all-gather(bf16[2,8,64,3,3]{2,1,4,3,0:T(8,128)(2,1)} %param.6), channel_id=1, replica_groups=mesh['gz'=32,'ch'=8] {'ch'}, dimensions={1}, use_global_device_ids=true | all-gather | bytes 165888 | tf_op jit(solution)/shard_map/all_gather | solution.py:29
  58.9 0.0 all-to-all-done.1
  58.9 3.4 %all-to-all-start = ((bf16[8,32,512]{2,0,1:T(8,128)(2,1)}), bf16[8,32,512]{2,0,1:T(8,128)(2,1)S(1)}, u32[]{:S(2)}, u32[]{:S(2)}) async-start(bf16[8,32,512]{2,0,1:T(8,128)(2,1)} %copy.37), calls=%async_computation | async-start | bytes 524288 | tf_op jit(solution)/shard_map/all_to_all | solution.py:62
  62.4 0.2 reshape.27
  62.7 6.9 %all-to-all-done = bf16[8,32,512]{2,0,1:T(8,128)(2,1)S(1)} async-done(((bf16[8,32,512]{2,0,1:T(8,128)(2,1)}), bf16[8,32,512]{2,0,1:T(8,128)(2,1)S(1)}, u32[]{:S(2)}, u32[]{:S(2)}) %all-to-all-start) | async-done | bytes 262176 | tf_op jit(solution)/shard_map/all_to_all | solution.py:62
  69.6 5.9 %reshape.17 = bf16[64,4,64,8]{3,2,0,1:T(8,128)(2,1)} reshape(bf16[8,8,4,512]{3,1,0,2:T(8,128)(2,1)S(1)} %bitcast.87) | data formatting | bytes 524288 | tf_op jit(solution)/shard_map/reshape | solution.py:64
  75.5 5.8 %copy.40 = bf16[64,4,64,8]{0,1,3,2:T(4,128)(2,1)S(1)} copy(bf16[64,4,64,8]{3,2,0,1:T(8,128)(2,1)} %reshape.17) | data formatting | bytes 524288 | tf_op jit(solution)/shard_map/reshape | solution.py:64
  81.3 5.5 %fusion.5 = bf16[64,4,64,8]{0,1,3,2:T(4,128)(2,1)S(1)} fusion(bf16[64,4,64,8]{0,1,3,2:T(4,128)(2,1)S(1)} %copy.40, bf16[2,64,64,3,3]{2,1,4,3,0:T(8,128)(2,1)S(1)} %all_gather.6, bf16[1,8,8,64,3,3]{3,2,5,4,0,1:T(8,128)(2,1)S(1)} %get-tuple-element.6), kind=kOutput, calls=%fused_computation.13 | convolution fusion | flops 274464768 | bytes 1081344 | tf_op jit(solution)/shard_map/conv_general_dilated | solution.py:35
  86.8 4.8 %collective-permute-start = (bf16[64,4,64,8]{0,1,3,2:T(4,128)(2,1)S(1)}, bf16[64,4,64,8]{0,1,3,2:T(4,128)(2,1)S(1)}, u32[]{:S(2)}, u32[]{:S(2)}) collective-permute-start(bf16[64,4,64,8]{0,1,3,2:T(4,128)(2,1)S(1)} %fusion.5), channel_id=1, source_target_pairs={{0,16},{8,24},{16,32},{24,40},{32,48},{40,56},{48,64},{56,72},{64,... | collective-permute-start | bytes 786440 | tf_op jit(solution)/shard_map/ppermute | solution.py:23
  91.7 4.8 %collective-permute-start.1 = (bf16[64,4,64,8]{0,1,3,2:T(4,128)(2,1)S(1)}, bf16[64,4,64,8]{0,1,3,2:T(4,128)(2,1)S(1)}, u32[]{:S(2)}, u32[]{:S(2)}) collective-permute-start(bf16[64,4,64,8]{0,1,3,2:T(4,128)(2,1)S(1)} %fusion.5), channel_id=1, source_target_pairs={{16,0},{24,8},{32,16},{40,24},{48,32},{56,40},{64,48},{72,56},{80,... | collective-permute-start | bytes 786440 | tf_op jit(solution)/shard_map/ppermute | solution.py:23
  96.5 0.4 fusion.16
  96.9 7.1 %collective-permute-done = bf16[64,4,64,8]{0,1,3,2:T(4,128)(2,1)S(1)} collective-permute-done((bf16[64,4,64,8]{0,1,3,2:T(4,128)(2,1)S(1)}, bf16[64,4,64,8]{0,1,3,2:T(4,128)(2,1)S(1)}, u32[]{:S(2)}, u32[]{:S(2)}) %collective-permute-start) | collective-permute-done | bytes 262176 | tf_op jit(solution)/shard_map/ppermute | solution.py:23
  104.0 0.4 convolution_add_fusion.3
  104.4 2.8 %collective-permute-done.1 = bf16[64,4,64,8]{0,1,3,2:T(4,128)(2,1)S(1)} collective-permute-done((bf16[64,4,64,8]{0,1,3,2:T(4,128)(2,1)S(1)}, bf16[64,4,64,8]{0,1,3,2:T(4,128)(2,1)S(1)}, u32[]{:S(2)}, u32[]{:S(2)}) %collective-permute-start.1) | collective-permute-done | bytes 262176 | tf_op jit(solution)/shard_map/ppermute | solution.py:23
  107.1 0.4 fusion.2
  107.6 5.6 %fusion.7 = bf16[64,4,64,8]{0,1,3,2:T(4,128)(2,1)S(1)} fusion(bf16[4,64,8,64]{3,1,2,0:T(8,128)(2,1)S(1)} %fusion.2, bf16[2,64,64,3,3]{2,1,4,3,0:T(8,128)(2,1)S(1)} %all_gather.6, bf16[1,8,8,64,3,3]{3,2,5,4,0,1:T(8,128)(2,1)S(1)} %get-tuple-element.5), kind=kOutput, calls=%fused_computation.15 | convolution fusion | flops 274464768 | bytes 1081344 | tf_op jit(solution)/shard_map/conv_general_dilated | solution.py:35
  113.2 3.1 %collective-permute-start.2 = (bf16[64,4,64,8]{0,1,3,2:T(4,128)(2,1)S(1)}, bf16[64,4,64,8]{0,1,3,2:T(4,128)(2,1)S(1)}, u32[]{:S(2)}, u32[]{:S(2)}) collective-permute-start(bf16[64,4,64,8]{0,1,3,2:T(4,128)(2,1)S(1)} %fusion.7), channel_id=1, source_target_pairs={{0,16},{8,24},{16,32},{24,40},{32,48},{40,56},{48,64},{56,72},{64,... | collective-permute-start | bytes 786440 | tf_op jit(solution)/shard_map/ppermute | solution.py:23
  116.3 6.3 %collective-permute-start.3 = (bf16[64,4,64,8]{0,1,3,2:T(4,128)(2,1)S(1)}, bf16[64,4,64,8]{0,1,3,2:T(4,128)(2,1)S(1)}, u32[]{:S(2)}, u32[]{:S(2)}) collective-permute-start(bf16[64,4,64,8]{0,1,3,2:T(4,128)(2,1)S(1)} %fusion.7), channel_id=1, source_target_pairs={{16,0},{24,8},{32,16},{40,24},{48,32},{56,40},{64,48},{72,56},{80,... | collective-permute-start | bytes 786440 | tf_op jit(solution)/shard_map/ppermute | solution.py:23
  122.7 0.4 fusion.11
  123.1 7.0 %collective-permute-done.2 = bf16[64,4,64,8]{0,1,3,2:T(4,128)(2,1)S(1)} collective-permute-done((bf16[64,4,64,8]{0,1,3,2:T(4,128)(2,1)S(1)}, bf16[64,4,64,8]{0,1,3,2:T(4,128)(2,1)S(1)}, u32[]{:S(2)}, u32[]{:S(2)}) %collective-permute-start.2) | collective-permute-done | bytes 262176 | tf_op jit(solution)/shard_map/ppermute | solution.py:23
  130.0 0.4 convolution_add_fusion.1
  130.4 4.5 %collective-permute-done.3 = bf16[64,4,64,8]{0,1,3,2:T(4,128)(2,1)S(1)} collective-permute-done((bf16[64,4,64,8]{0,1,3,2:T(4,128)(2,1)S(1)}, bf16[64,4,64,8]{0,1,3,2:T(4,128)(2,1)S(1)}, u32[]{:S(2)}, u32[]{:S(2)}) %collective-permute-start.3) | collective-permute-done | bytes 262176 | tf_op jit(solution)/shard_map/ppermute | solution.py:23
  134.9 0.4 fusion.8
  135.3 0.3 copy.89
  135.7 0.3 copy.50
  136.0 9.8 %all_to_all.38 = bf16[64,4,512]{2,1,0:T(4,128)(2,1)S(1)} all-to-all(bf16[64,4,512]{2,1,0:T(4,128)(2,1)S(1)} %copy.50), channel_id=1, replica_groups=mesh['gz'=32,'ch'=8] {'ch'}, dimensions={0} | all-to-all | bytes 524288 | tf_op jit(solution)/shard_map/all_to_all | solution.py:70
  145.9 0.8 copy.53
  (8 shorter events, 0.2 us)
Async XLA Ops:
  0.0 0.8 copy-start
  1.7 57.3 %all-to-all-start.1 = ((bf16[8,2,4608]{2,1,0:T(2,128)(2,1)}), bf16[8,2,4608]{2,1,0:T(2,128)(2,1)S(1)}, u32[]{:S(2)}, u32[]{:S(2)}) async-start(bf16[8,2,4608]{2,1,0:T(2,128)(2,1)} %reshape.26), calls=%async_computation.1 | async-start | bytes 294912 | tf_op jit(solution)/shard_map/all_to_all | solution.py:13
  58.9 10.6 %all-to-all-start = ((bf16[8,32,512]{2,0,1:T(8,128)(2,1)}), bf16[8,32,512]{2,0,1:T(8,128)(2,1)S(1)}, u32[]{:S(2)}, u32[]{:S(2)}) async-start(bf16[8,32,512]{2,0,1:T(8,128)(2,1)} %copy.37), calls=%async_computation | async-start | bytes 524288 | tf_op jit(solution)/shard_map/all_to_all | solution.py:62
  86.8 17.1 %collective-permute-start = (bf16[64,4,64,8]{0,1,3,2:T(4,128)(2,1)S(1)}, bf16[64,4,64,8]{0,1,3,2:T(4,128)(2,1)S(1)}, u32[]{:S(2)}, u32[]{:S(2)}) collective-permute-start(bf16[64,4,64,8]{0,1,3,2:T(4,128)(2,1)S(1)} %fusion.5), channel_id=1, source_target_pairs={{0,16},{8,24},{16,32},{24,40},{32,48},{40,56},{48,64},{56,72},{64,... | collective-permute-start | bytes 786440 | tf_op jit(solution)/shard_map/ppermute | solution.py:23
  91.7 15.5 %collective-permute-start.1 = (bf16[64,4,64,8]{0,1,3,2:T(4,128)(2,1)S(1)}, bf16[64,4,64,8]{0,1,3,2:T(4,128)(2,1)S(1)}, u32[]{:S(2)}, u32[]{:S(2)}) collective-permute-start(bf16[64,4,64,8]{0,1,3,2:T(4,128)(2,1)S(1)} %fusion.5), channel_id=1, source_target_pairs={{16,0},{24,8},{32,16},{40,24},{48,32},{56,40},{64,48},{72,56},{80,... | collective-permute-start | bytes 786440 | tf_op jit(solution)/shard_map/ppermute | solution.py:23
  113.2 16.8 %collective-permute-start.2 = (bf16[64,4,64,8]{0,1,3,2:T(4,128)(2,1)S(1)}, bf16[64,4,64,8]{0,1,3,2:T(4,128)(2,1)S(1)}, u32[]{:S(2)}, u32[]{:S(2)}) collective-permute-start(bf16[64,4,64,8]{0,1,3,2:T(4,128)(2,1)S(1)} %fusion.7), channel_id=1, source_target_pairs={{0,16},{8,24},{16,32},{24,40},{32,48},{40,56},{48,64},{56,72},{64,... | collective-permute-start | bytes 786440 | tf_op jit(solution)/shard_map/ppermute | solution.py:23
  116.3 18.6 %collective-permute-start.3 = (bf16[64,4,64,8]{0,1,3,2:T(4,128)(2,1)S(1)}, bf16[64,4,64,8]{0,1,3,2:T(4,128)(2,1)S(1)}, u32[]{:S(2)}, u32[]{:S(2)}) collective-permute-start(bf16[64,4,64,8]{0,1,3,2:T(4,128)(2,1)S(1)} %fusion.7), channel_id=1, source_target_pairs={{16,0},{24,8},{32,16},{40,24},{48,32},{56,40},{64,48},{72,56},{80,... | collective-permute-start | bytes 786440 | tf_op jit(solution)/shard_map/ppermute | solution.py:23
